TPU v7x, 256 devices: a whole 4x4x8 slice. The times are simulated.
256 devices in a mesh: tile: 16 (over z, core), tensor: 16 (over y, x).
Axes of the slice: x: 4, y: 4, z: 8, core: 2. Of those that a mesh axis runs over, the one named last changes fastest.
Arguments:
- image_hidden: bfloat16 [8, 32, 32, 3072], P(None, 'tile', 'tensor'), may hold values from -6 to 6
- text_hidden: bfloat16 [8, 512, 3072], P(None, ('tile', 'tensor')), may hold values from -6 to 6
- latents: float32 [8, 32, 2048], P(None, 'tile', 'tensor'), may hold values from -6 to 6
- step_index: int32 [8], replicated, may hold values from 0 to 27
- anchor: int32 [8, 2], replicated, may hold values from 0 to 63
- text_len: int32 [8], replicated, may hold values from 64 to 512
- mod_image: float32 [8, 3, 3072], replicated, may hold values from -3 to 3
- mod_text: float32 [8, 3, 3072], replicated, may hold values from -3 to 3
- mod_mlp: float32 [8, 3, 3072], replicated, may hold values from -3 to 3
- mod_final: float32 [8, 2, 3072], replicated, may hold values from -3 to 3
- qkv_image: bfloat16 [3072, 3, 2048], P(None, None, 'tensor'), may hold values from -0.109375 to 0.109375
- qkv_text: bfloat16 [3072, 3, 2048], P(None, None, 'tensor'), may hold values from -0.109375 to 0.109375
- proj_image: bfloat16 [2048, 3072], P('tensor'), may hold values from -0.125 to 0.125
- proj_text: bfloat16 [2048, 3072], P('tensor'), may hold values from -0.125 to 0.125
- qk_gain: float32 [2, 2, 128], replicated, may hold values from 0.5 to 10
- mlp_expand: bfloat16 [3072, 6144], P(None, 'tensor'), may hold values from -0.109375 to 0.109375
- mlp_reduce: bfloat16 [6144, 3072], P('tensor'), may hold values from -0.078125 to 0.078125
- final_weight: bfloat16 [3072, 64], replicated, may hold values from -0.109375 to 0.109375
Outputs:
- image_out: bfloat16 [8, 32, 32, 3072], P(None, 'tile', 'tensor')
- text_out: bfloat16 [8, 512, 3072], P(None, ('tile', 'tensor'))
- latents_ext: float32 [8, 64, 2048], P(None, 'tile', 'tensor')
Inputs may be any that keep to these rules, and one draw needn't show every extreme that they name: text_len gives each request's live text tokens; slots at or past it take no part as keys. step_index is a step of the 28-step plan.
All inputs are finite; a program needn't handle non-finite values.
Results may differ from a plain program's by a relative error of at most 0.0085.
The roundings to bfloat16 on the way count: a program that leaves them out, or rounds other values in their place, can miss the bound.
Values may be sent and summed in bfloat16 or wider, within the bound.
No kernel may reach another device: no remote copies, remote signals or barrier semaphores. Data moves between devices by JAX's collectives and lax.ppermute only.
A program may use at most 128 MiB of HBM per device.

v0:
```python
import math
import jax
import jax.numpy as jnp
from jax import lax
from jax.sharding import PartitionSpec as P

HEAD_DIM = 128
GRID = 32
NSTEPS = 28
norm_eps = 1e-06
time_shift = 3.0


def padded(value, sides, width):
    for axis, dim in sides:
        size, length = (lax.axis_size(axis), value.shape[dim])
        up = [(i, (i + 1) % size) for i in range(size - 1)]
        down = [(j, i) for i, j in up]
        last = lax.slice_in_dim(value, length - width, length, axis=dim)
        leading = lax.slice_in_dim(value, 0, width, axis=dim)
        before = lax.ppermute(last, axis, up)
        after = lax.ppermute(leading, axis, down)
        value = jnp.concatenate([before, value, after], axis=dim)
    return value


def layer_norm(values):
    average = jnp.mean(values, -1, keepdims=True)
    centred = values - average
    spread = jnp.mean(centred * centred, -1, keepdims=True)
    return centred * lax.rsqrt(spread + norm_eps)


def modulate(hidden, shift, stretch):
    normed = layer_norm(hidden.astype(jnp.float32))
    return ((1.0 + stretch) * normed + shift).astype(jnp.bfloat16)


def rope_tables(row_ids, col_ids):
    lane = jnp.arange(2 * 64, dtype=jnp.int32)
    pair_index = lane // 2
    row_rank = (pair_index - 8).astype(jnp.float32)
    col_rank = (pair_index - 36).astype(jnp.float32)
    log_base = math.log(10000.0)
    row_freq = jnp.where(
        (pair_index >= 8) & (pair_index < 36), jnp.exp(-2.0 * row_rank / 56.0 * log_base), 0.0
    )
    col_freq = jnp.where(pair_index >= 36, jnp.exp(-2.0 * col_rank / 56.0 * log_base), 0.0)
    angles = row_ids[..., None] * row_freq + col_ids[..., None] * col_freq
    sign_table = jnp.where(lane % 2 == 0, -1.0, 1.0).astype(jnp.float32)
    return (jnp.cos(angles), jnp.sin(angles) * sign_table)


def rotate(values, cos_table, sin_table):
    lane = lax.broadcasted_iota(jnp.int32, values.shape, values.ndim - 1)
    swapped = jnp.where(lane % 2 == 0, jnp.roll(values, -1, axis=-1), jnp.roll(values, 1, axis=-1))
    return values * cos_table + swapped * sin_table


def head_norm(projected, head_gain):
    squares = jnp.mean(projected * projected, -1, keepdims=True)
    return projected * lax.rsqrt(squares + norm_eps) * head_gain


def sigma_of(step_float):
    level = 1.0 - step_float / NSTEPS
    return time_shift * level / (1.0 + (time_shift - 1.0) * level)


def key_usable(text_len, key_count, text_tile, block_len):
    key_pos = jnp.arange(key_count, dtype=jnp.int32)
    owner_tile = key_pos // block_len
    offset = key_pos % block_len
    text_pos = owner_tile * text_tile + offset
    return jnp.logical_or(offset[None, :] >= text_tile, text_pos[None, :] < text_len[:, None])


def sum_over_tensor(term, owners, narrow):
    if not narrow:
        return lax.psum_scatter(term, "tensor", scatter_dimension=0, tiled=True)
    parts = term.astype(jnp.bfloat16).reshape((owners, -1) + term.shape[1:])
    parts = lax.all_to_all(parts, "tensor", 0, 0, tiled=True)
    return jnp.sum(parts.astype(jnp.float32), 0)


NARROW_SUMS = True


def per_device(
    image_hidden,
    text_hidden,
    latents,
    step_index,
    anchor,
    text_len,
    mod_image,
    mod_text,
    mod_mlp,
    mod_final,
    qkv_image,
    qkv_text,
    proj_image,
    proj_text,
    qk_gain,
    mlp_expand,
    mlp_reduce,
    final_weight,
):
    requests, tile_rows, tile_cols, model_width = image_hidden.shape
    local_cols = qkv_image.shape[2]
    local_heads = local_cols // HEAD_DIM
    owners = lax.axis_size("tensor")
    own_image = tile_rows * tile_cols
    own_text = text_hidden.shape[1]
    slots = own_image + own_text
    image_own = image_hidden.reshape(requests, own_image, model_width).transpose(1, 0, 2)
    text_own = text_hidden.transpose(1, 0, 2)
    image_mod_own = modulate(image_own, mod_image[None, :, 0, :], mod_image[None, :, 1, :])
    text_mod_own = modulate(text_own, mod_text[None, :, 0, :], mod_text[None, :, 1, :])
    image_count = owners * own_image
    text_tile = owners * own_text
    block_len = text_tile + image_count
    image_mod = lax.all_gather(image_mod_own, "tensor", axis=0, tiled=True).reshape(
        image_count * requests, model_width
    )
    text_mod = lax.all_to_all(
        jnp.broadcast_to(text_mod_own[None], (owners,) + text_mod_own.shape),
        "tensor",
        0,
        0,
        tiled=True,
    ).reshape(text_tile * requests, model_width)
    tile_index = lax.axis_index("tile")
    token_index = jnp.arange(image_count, dtype=jnp.int32)
    owner = token_index // own_image
    within = token_index % own_image
    row_ids = (anchor[None, :, 0] + tile_index * tile_rows + (within // tile_cols)[:, None]).astype(
        jnp.float32
    )
    col_ids = (anchor[None, :, 1] + (owner * tile_cols + within % tile_cols)[:, None]).astype(
        jnp.float32
    )
    cos_table, sin_table = rope_tables(row_ids.reshape(-1), col_ids.reshape(-1))
    cos_table = cos_table[:, None, :]
    sin_table = sin_table[:, None, :]
    image_qkv = jnp.dot(
        image_mod,
        qkv_image.reshape(model_width, 3 * local_cols),
        preferred_element_type=jnp.float32,
    ).reshape(image_count * requests, 3, local_heads, HEAD_DIM)
    text_qkv = jnp.dot(
        text_mod, qkv_text.reshape(model_width, 3 * local_cols), preferred_element_type=jnp.float32
    ).reshape(text_tile * requests, 3, local_heads, HEAD_DIM)
    token_shape = (block_len, requests, local_heads, HEAD_DIM)
    query = jnp.concatenate(
        [
            head_norm(text_qkv[:, 0], qk_gain[1, 0]).astype(jnp.bfloat16),
            rotate(head_norm(image_qkv[:, 0], qk_gain[0, 0]), cos_table, sin_table).astype(
                jnp.bfloat16
            ),
        ],
        0,
    ).reshape(token_shape)
    keys = jnp.concatenate(
        [
            head_norm(text_qkv[:, 1], qk_gain[1, 1]).astype(jnp.bfloat16),
            rotate(head_norm(image_qkv[:, 1], qk_gain[0, 1]), cos_table, sin_table).astype(
                jnp.bfloat16
            ),
        ],
        0,
    ).reshape(token_shape)
    values = (
        jnp.concatenate([text_qkv[:, 2], image_qkv[:, 2]], 0)
        .astype(jnp.bfloat16)
        .reshape(token_shape)
    )
    score_scale = 1.0 / math.sqrt(HEAD_DIM)
    tiles = lax.axis_size("tile")
    parts = tiles // requests
    part_len = block_len // parts
    keys_r = jnp.repeat(keys.transpose(1, 0, 2, 3), parts, axis=0)
    values_r = jnp.repeat(values.transpose(1, 0, 2, 3), parts, axis=0)
    query_r = query.transpose(1, 0, 2, 3).reshape(tiles, part_len, local_heads, HEAD_DIM)
    outgoing = jnp.concatenate([keys_r, values_r, query_r], 1)
    incoming = lax.all_to_all(outgoing, "tile", 0, 0, tiled=True)
    keys_all = incoming[:, :block_len].reshape(tiles * block_len, local_heads, HEAD_DIM)
    values_all = incoming[:, block_len : 2 * block_len].reshape(
        tiles * block_len, local_heads, HEAD_DIM
    )
    query_mine = incoming[:, 2 * block_len :].reshape(tiles * part_len, local_heads, HEAD_DIM)
    my_request = tile_index // parts
    usable = key_usable(text_len[my_request][None], keys_all.shape[0], text_tile, block_len)[0][
        None, None, :
    ]
    scores = (
        jnp.einsum("qhd,khd->hqk", query_mine, keys_all, preferred_element_type=jnp.float32)
        * score_scale
    )
    row_top = jnp.max(jnp.where(usable, scores, -jnp.inf), -1, keepdims=True)
    weights_raw = jnp.where(usable, jnp.exp(scores - row_top), 0.0)
    weight_sum = jnp.sum(weights_raw, -1, keepdims=True)
    accum = jnp.einsum(
        "hqk,khd->hqd",
        weights_raw.astype(jnp.bfloat16),
        values_all,
        preferred_element_type=jnp.float32,
    )
    attended_mine = (
        (accum / weight_sum)
        .astype(jnp.bfloat16)
        .transpose(1, 0, 2)
        .reshape(tiles, part_len, local_heads * HEAD_DIM)
    )
    returned = lax.all_to_all(attended_mine, "tile", 0, 0, tiled=True)
    attended = returned.reshape(requests, block_len, local_cols).transpose(1, 0, 2)
    text_att = attended[:text_tile].reshape(text_tile * requests, local_cols)
    image_att = attended[text_tile:].reshape(image_count * requests, local_cols)
    image_term = jnp.dot(image_att, proj_image, preferred_element_type=jnp.float32).reshape(
        image_count, requests, model_width
    )
    image_sum = sum_over_tensor(image_term, owners, NARROW_SUMS)
    text_term = jnp.dot(text_att, proj_text, preferred_element_type=jnp.float32).reshape(
        text_tile, requests, model_width
    )
    after_image = (image_sum[0, 0, 0] * 0.0).astype(text_term.dtype)
    text_sum = sum_over_tensor(text_term + after_image, owners, NARROW_SUMS)
    image_mid = (image_own.astype(jnp.float32) + mod_image[None, :, 2, :] * image_sum).astype(
        jnp.bfloat16
    )
    mlp_mod = modulate(image_mid, mod_mlp[None, :, 0, :], mod_mlp[None, :, 1, :])
    piece = lax.all_gather(mlp_mod, "tensor", axis=0, tiled=True)
    grown = jnp.dot(piece.reshape(-1, model_width), mlp_expand, preferred_element_type=jnp.float32)
    activated = jax.nn.gelu(grown, approximate=True).astype(jnp.bfloat16)
    text_out = (text_own.astype(jnp.float32) + mod_text[None, :, 2, :] * text_sum).astype(
        jnp.bfloat16
    )
    mlp_term = jnp.dot(activated, mlp_reduce, preferred_element_type=jnp.float32).reshape(
        image_count, requests, model_width
    )
    mlp_sum = sum_over_tensor(mlp_term, owners, NARROW_SUMS)
    image_out = (image_mid.astype(jnp.float32) + mod_mlp[None, :, 2, :] * mlp_sum).astype(
        jnp.bfloat16
    )
    final_in = modulate(image_out, mod_final[None, :, 0, :], mod_final[None, :, 1, :])
    velocity = jnp.dot(
        final_in.reshape(own_image * requests, model_width),
        final_weight,
        preferred_element_type=jnp.float32,
    ).reshape(own_image, requests, final_weight.shape[1])
    velocity = velocity.transpose(1, 0, 2).reshape(
        requests, tile_rows, tile_cols * final_weight.shape[1]
    )
    step_float = step_index.astype(jnp.float32)
    time_delta = sigma_of(step_float + 1.0) - sigma_of(step_float)
    latents_next = latents + time_delta[:, None, None] * velocity
    latents_ext = padded(latents_next, (("tile", 1),), 1)
    image_out = image_out.transpose(1, 0, 2).reshape(requests, tile_rows, tile_cols, model_width)
    return (image_out, text_out.transpose(1, 0, 2), latents_ext)


def solution(mesh):
    return jax.shard_map(
        per_device,
        mesh=mesh,
        in_specs=(
            P(None, "tile", "tensor", None),
            P(None, ("tile", "tensor"), None),
            P(None, "tile", "tensor"),
            P(),
            P(),
            P(),
            P(),
            P(),
            P(),
            P(),
            P(None, None, "tensor"),
            P(None, None, "tensor"),
            P("tensor", None),
            P("tensor", None),
            P(),
            P(None, "tensor"),
            P("tensor", None),
            P(),
        ),
        out_specs=(
            P(None, "tile", "tensor", None),
            P(None, ("tile", "tensor"), None),
            P(None, "tile", "tensor"),
        ),
        check_vma=False,
    )
```

profile of v0, /device:TPU:97, one launch (start us, length us, event | category | flops | bytes accessed | tf_op | source)
XLA Modules:
  0.0 343.5 jit_solution(16405498130412113823)
XLA Ops:
  7.2 1.1 copy.54
  8.7 1.0 slice_bitcast_fusion.9
  9.7 0.8 add_convert_fusion.1
  10.6 1.0 fusion.66
  11.8 0.7 slice_bitcast_fusion.4
  12.6 1.3 broadcast_in_dim.42
  13.9 6.8 %all-to-all-start = ((bf16[16,2,8,3072]{3,2,1,0:T(8,128)(2,1)}), bf16[16,2,8,3072]{3,2,1,0:T(8,128)(2,1)}, u32[]{:S(2)}, u32[]{:S(2)}) async-start(bf16[16,2,8,3072]{3,2,1,0:T(8,128)(2,1)} %broadcast_in_dim.42), calls=%async_computation | async-start | bytes 3145728 | tf_op jit(solution)/shard_map/all_to_all | solution.py:126
  20.7 4.3 %copy.57 = bf16[3072,3,128]{0,2,1:T(8,128)(2,1)} copy(bf16[3072,3,128]{2,0,1:T(8,128)(2,1)} %param.28) | data formatting | bytes 4718592 | tf_op args[10]
  25.3 4.3 %copy.56 = bf16[3072,3,128]{0,2,1:T(8,128)(2,1)} copy(bf16[3072,3,128]{2,0,1:T(8,128)(2,1)} %param.29) | data formatting | bytes 4718592 | tf_op args[11]
  29.6 0.6 and_select_fusion.2
  30.2 0.5 compare_and_fusion
  30.8 0.6 compare_select_fusion
  31.3 0.6 iota_and_fusion
  31.9 14.3 %all-to-all-done = bf16[16,2,8,3072]{3,2,1,0:T(8,128)(2,1)} async-done(((bf16[16,2,8,3072]{3,2,1,0:T(8,128)(2,1)}), bf16[16,2,8,3072]{3,2,1,0:T(8,128)(2,1)}, u32[]{:S(2)}, u32[]{:S(2)}) %all-to-all-start) | async-done | bytes 1572896 | tf_op jit(solution)/shard_map/all_to_all | solution.py:126
  46.2 3.1 fusion.13
  49.8 0.7 copy.65
  50.5 0.7 copy.62
  51.3 24.4 %all-gather.3.cloned.1.call-done = bf16[64,8,3072]{2,1,0:T(8,128)(2,1)} async-done(((bf16[4,8,3072]{2,1,0:T(8,128)(2,1)}), bf16[64,8,3072]{2,1,0:T(8,128)(2,1)}) %all-gather.3.cloned.1.call-update) | async-done | bytes 3145744 | tf_op jit(solution)/shard_map/all_gather | solution.py:123
  75.7 4.0 %fusion.3 = f32[512,3,128]{0,2,1:T(8,128)S(1)} fusion(bf16[64,8,3072]{2,1,0:T(8,128)(2,1)} %all-gather.3.cloned.1.call-done, bf16[3072,3,128]{0,2,1:T(8,128)(2,1)} %copy.57), kind=kOutput, calls=%fused_computation.10 | convolution fusion | flops 1207959552 | bytes 6291456 | tf_op jit(solution)/shard_map/dot_general | solution.py:146
  80.2 0.7 fusion.83
  80.9 2.1 fusion.60
  83.2 0.9 pad_maximum_fusion.3
  84.3 0.7 copy.67
  85.0 0.9 pad_maximum_fusion.2
  86.3 2.0 pad_maximum_fusion
  88.3 7.9 %all-to-all-start.1 = ((bf16[16,240,1,128]{3,1,2,0:T(8,128)(2,1)}), bf16[16,240,1,128]{3,1,2,0:T(8,128)(2,1)}, u32[]{:S(2)}, u32[]{:S(2)}) async-start(bf16[16,240,1,128]{3,1,2,0:T(8,128)(2,1)} %pad_maximum_fusion), calls=%async_computation.1 | async-start | bytes 1966080 | tf_op jit(solution)/shard_map/all_to_all | solution.py:186
  96.2 0.6 dynamic_slice.3
  96.8 0.7 fusion.95
  97.5 23.7 %all-to-all-done.1 = bf16[16,240,1,128]{3,1,2,0:T(8,128)(2,1)} async-done(((bf16[16,240,1,128]{3,1,2,0:T(8,128)(2,1)}), bf16[16,240,1,128]{3,1,2,0:T(8,128)(2,1)}, u32[]{:S(2)}, u32[]{:S(2)}) %all-to-all-start.1) | async-done | bytes 983072 | tf_op jit(solution)/shard_map/all_to_all | solution.py:186
  121.1 1.2 fusion.105
  122.3 0.9 slice.176
  123.2 0.9 select_reduce_fusion
  124.1 1.1 fusion.1
  125.2 0.9 fusion.19
  126.1 13.0 %all_to_all.30 = bf16[16,48,128]{2,1,0:T(8,128)(2,1)S(1)} all-to-all(bf16[16,48,128]{2,1,0:T(8,128)(2,1)S(1)} %bitcast.211), channel_id=1, replica_groups=mesh['tile'=16,'tensor'=16] {'tile'}, dimensions={0} | all-to-all | bytes 393216 | tf_op jit(solution)/shard_map/all_to_all | solution.py:215
  139.1 0.7 copy-done.3
  139.8 2.6 convolution_convert_fusion
  142.5 4.6 %all-to-all-start.3 = ((bf16[16,4,8,3072]{3,2,1,0:T(8,128)(2,1)}), bf16[16,4,8,3072]{3,2,1,0:T(8,128)(2,1)}, u32[]{:S(2)}, u32[]{:S(2)}) async-start(bf16[16,4,8,3072]{3,2,1,0:T(8,128)(2,1)} %bitcast.191), calls=%async_computation.3 | async-start | bytes 6291456 | tf_op jit(solution)/shard_map/all_to_all | solution.py:82
  147.1 0.2 all-gather.5.cloned.1.call-start
  147.3 0.7 slice_bitcast_fusion.6
  148.0 46.9 %all-to-all-done.3 = bf16[16,4,8,3072]{3,2,1,0:T(8,128)(2,1)} async-done(((bf16[16,4,8,3072]{3,2,1,0:T(8,128)(2,1)}), bf16[16,4,8,3072]{3,2,1,0:T(8,128)(2,1)}, u32[]{:S(2)}, u32[]{:S(2)}) %all-to-all-start.3) | async-done | bytes 3145760 | tf_op jit(solution)/shard_map/all_to_all | solution.py:82
  194.9 2.5 convert_reduce_fusion.1
  197.6 0.2 fusion.42
  197.9 0.8 fusion.45
  198.7 0.5 slice.179
  199.9 3.0 fusion
  202.9 4.4 %all-to-all-start.5 = ((bf16[16,2,8,3072]{3,2,1,0:T(8,128)(2,1)}), bf16[16,2,8,3072]{3,2,1,0:T(8,128)(2,1)}, u32[]{:S(2)}, u32[]{:S(2)}) async-start(bf16[16,2,8,3072]{3,2,1,0:T(8,128)(2,1)} %bitcast.192), calls=%async_computation.5 | async-start | bytes 3145728 | tf_op jit(solution)/shard_map/all_to_all | solution.py:82
  207.3 52.4 %all-gather.5.cloned.1.call-done = bf16[64,8,3072]{2,1,0:T(8,128)(2,1)} async-done(((bf16[4,8,3072]{2,1,0:T(8,128)(2,1)}), bf16[64,8,3072]{2,1,0:T(8,128)(2,1)}) %all-gather.5.cloned.1.call-update) | async-done | bytes 3145744 | tf_op jit(solution)/shard_map/all_gather | solution.py:232
  259.7 7.8 %convolution_convert_fusion.1 = bf16[512,3072]{1,0:T(8,128)(2,1)} fusion(bf16[384,3072]{1,0:T(8,128)(2,1)S(1)} %copy-done, bf16[3072,384]{1,0:T(8,128)(2,1)} %param.33, bf16[64,8,3072]{2,1,0:T(8,128)(2,1)} %all-gather.5.cloned.1.call-done), kind=kOutput, calls=%fused_computation.5 | convolution fusion | flops 2419261440 | bytes 11010048 | tf_op jit(solution)/shard_map/dot_general | solution.py:238
  267.5 4.6 %all-to-all-start.4 = ((bf16[16,4,8,3072]{3,2,1,0:T(8,128)(2,1)}), bf16[16,4,8,3072]{3,2,1,0:T(8,128)(2,1)}, u32[]{:S(2)}, u32[]{:S(2)}) async-start(bf16[16,4,8,3072]{3,2,1,0:T(8,128)(2,1)} %bitcast.193), calls=%async_computation.4 | async-start | bytes 6291456 | tf_op jit(solution)/shard_map/all_to_all | solution.py:82
  272.2 1.2 fusion.110
  273.4 0.7 copy_bitcast_fusion
  274.1 1.6 convert_reduce_fusion.2
  275.8 0.7 copy.74
  276.6 41.8 %all-to-all-done.4 = bf16[16,4,8,3072]{3,2,1,0:T(8,128)(2,1)} async-done(((bf16[16,4,8,3072]{3,2,1,0:T(8,128)(2,1)}), bf16[16,4,8,3072]{3,2,1,0:T(8,128)(2,1)}, u32[]{:S(2)}, u32[]{:S(2)}) %all-to-all-start.4) | async-done | bytes 3145760 | tf_op jit(solution)/shard_map/all_to_all | solution.py:82
  318.4 2.5 convert_reduce_fusion
  320.9 1.0 convert_reduce_fusion.4
  322.2 1.3 convolution_bitcast_fusion
  323.7 6.2 %collective-permute-start = (f32[8,1,128]{2,1,0:T(1,128)S(1)}, f32[8,1,128]{2,1,0:T(1,128)S(1)}, u32[]{:S(2)}, u32[]{:S(2)}) collective-permute-start(f32[8,1,128]{2,1,0:T(1,128)S(1)} %get-tuple-element.33), channel_id=1, source_target_pairs={{0,16},{16,32},{32,48},{48,64},{64,80},{80,96},{96,112},{112,128},... | collective-permute-start | bytes 12296 | tf_op jit(solution)/shard_map/ppermute | solution.py:21
  329.9 1.9 collective-permute-start.1
  331.9 1.1 fusion.52
  332.9 0.9 copy.73
  333.8 2.2 collective-permute-done.1
  336.1 0.6 pad_maximum_fusion.4
  (100 shorter events, 3.1 us)
Async XLA Ops:
  7.2 252.6 %copy-start = (bf16[384,3072]{1,0:T(8,128)(2,1)S(1)}, bf16[384,3072]{1,0:T(8,128)(2,1)}, u32[]{:S(2)}) copy-start(bf16[384,3072]{1,0:T(8,128)(2,1)} %param.34) | copy-start | bytes 7077892
  7.2 4.4 %copy-start.2 = (bf16[8,2,3072]{2,1,0:T(2,128)(2,1)S(1)}, bf16[8,2,3072]{2,1,0:T(2,128)(2,1)}, u32[]{:S(2)}) copy-start(bf16[8,2,3072]{2,1,0:T(2,128)(2,1)} %param.19) | copy-start | bytes 294916
  7.2 4.6 %copy-start.10 = (f32[8,3,3072]{2,0,1:T(8,128)S(1)}, f32[8,3,3072]{2,0,1:T(8,128)}, u32[]{:S(2)}) copy-start(f32[8,3,3072]{2,0,1:T(8,128)} %param.25) | copy-start | bytes 884740
  7.2 68.5 %all-gather.3.cloned.1.call-start = ((), (), s32[]{:S(2)}) async-start(), calls=%async_computation.6 | async-start | bytes 3342336 | tf_op jit(solution)/shard_map/all_gather | solution.py:123
  13.9 32.3 %all-to-all-start = ((bf16[16,2,8,3072]{3,2,1,0:T(8,128)(2,1)}), bf16[16,2,8,3072]{3,2,1,0:T(8,128)(2,1)}, u32[]{:S(2)}, u32[]{:S(2)}) async-start(bf16[16,2,8,3072]{3,2,1,0:T(8,128)(2,1)} %broadcast_in_dim.42), calls=%async_computation | async-start | bytes 3145728 | tf_op jit(solution)/shard_map/all_to_all | solution.py:126
  20.7 4.3 %copy-start.14 = (s32[8,2]{0,1:T(2,128)S(1)}, s32[8,2]{0,1:T(2,128)}, u32[]{:S(2)}) copy-start(s32[8,2]{0,1:T(2,128)} %param.22) | copy-start | bytes 196
  25.0 6.9 %copy-start.13 = (f32[2,2,128]{2,1,0:T(2,128)S(1)}, f32[2,2,128]{2,1,0:T(2,128)}, u32[]{:S(2)}) copy-start(f32[2,2,128]{2,1,0:T(2,128)} %param.32) | copy-start | bytes 6148
  79.7 1.1 copy-start.15
  79.8 1.1 copy-start.16
  79.8 1.1 copy-start.17
  79.8 1.1 copy-start.18
  79.8 1.0 copy-start.19
  79.8 1.0 copy-start.20
  85.0 11.2 %copy-start.21 = (s32[8]{0:T(128)S(1)}, s32[8]{0:T(128)}, u32[]{:S(2)}) copy-start(s32[8]{0:T(128)} %param.23) | copy-start | bytes 100
  88.3 32.8 %all-to-all-start.1 = ((bf16[16,240,1,128]{3,1,2,0:T(8,128)(2,1)}), bf16[16,240,1,128]{3,1,2,0:T(8,128)(2,1)}, u32[]{:S(2)}, u32[]{:S(2)}) async-start(bf16[16,240,1,128]{3,1,2,0:T(8,128)(2,1)} %pad_maximum_fusion), calls=%async_computation.1 | async-start | bytes 1966080 | tf_op jit(solution)/shard_map/all_to_all | solution.py:186
  125.2 14.6 %copy-start.4 = (bf16[128,3072]{1,0:T(8,128)(2,1)S(1)}, bf16[128,3072]{1,0:T(8,128)(2,1)}, u32[]{:S(2)}) copy-start(bf16[128,3072]{1,0:T(8,128)(2,1)} %param.30) | copy-start | bytes 2359300
  139.1 0.7 copy-start.3
  142.5 4.9 %copy-start.11 = (f32[8,3,3072]{2,0,1:T(8,128)S(1)}, f32[8,3,3072]{2,0,1:T(8,128)}, u32[]{:S(2)}) copy-start(f32[8,3,3072]{2,0,1:T(8,128)} %param.26) | copy-start | bytes 884740
  142.5 52.5 %all-to-all-start.3 = ((bf16[16,4,8,3072]{3,2,1,0:T(8,128)(2,1)}), bf16[16,4,8,3072]{3,2,1,0:T(8,128)(2,1)}, u32[]{:S(2)}, u32[]{:S(2)}) async-start(bf16[16,4,8,3072]{3,2,1,0:T(8,128)(2,1)} %bitcast.191), calls=%async_computation.3 | async-start | bytes 6291456 | tf_op jit(solution)/shard_map/all_to_all | solution.py:82
  147.1 112.6 %all-gather.5.cloned.1.call-start = ((), (), s32[]{:S(2)}) async-start(), calls=%async_computation.7 | async-start | bytes 3342336 | tf_op jit(solution)/shard_map/all_gather | solution.py:232
  194.9 3.0 copy-start.5
  194.9 3.0 copy-start.6
  197.5 5.4 %copy-start.1 = (f32[4,8,3072]{2,1,0:T(8,128)}, f32[4,8,3072]{2,1,0:T(8,128)S(1)}, u32[]{:S(2)}) copy-start(f32[4,8,3072]{2,1,0:T(8,128)S(1)} %convert_reduce_fusion.1) | copy-start | bytes 1179652
  202.9 64.6 %all-to-all-start.5 = ((bf16[16,2,8,3072]{3,2,1,0:T(8,128)(2,1)}), bf16[16,2,8,3072]{3,2,1,0:T(8,128)(2,1)}, u32[]{:S(2)}, u32[]{:S(2)}) async-start(bf16[16,2,8,3072]{3,2,1,0:T(8,128)(2,1)} %bitcast.192), calls=%async_computation.5 | async-start | bytes 3145728 | tf_op jit(solution)/shard_map/all_to_all | solution.py:82
  267.5 4.7 %copy-start.22 = (s32[8]{0:T(128)S(1)}, s32[8]{0:T(128)}, u32[]{:S(2)}) copy-start(s32[8]{0:T(128)} %param.21) | copy-start | bytes 100
  267.5 8.2 %copy-start.9 = (f32[8,3072]{1,0:T(8,128)S(1)}, f32[8,3072]{1,0:T(8,128)}, u32[]{:S(2)}) copy-start(f32[8,3072]{1,0:T(8,128)} %get-tuple-element.14) | copy-start | bytes 294916
  267.5 50.9 %all-to-all-start.4 = ((bf16[16,4,8,3072]{3,2,1,0:T(8,128)(2,1)}), bf16[16,4,8,3072]{3,2,1,0:T(8,128)(2,1)}, u32[]{:S(2)}, u32[]{:S(2)}) async-start(bf16[16,4,8,3072]{3,2,1,0:T(8,128)(2,1)} %bitcast.193), calls=%async_computation.4 | async-start | bytes 6291456 | tf_op jit(solution)/shard_map/all_to_all | solution.py:82
  275.7 47.8 %copy-start.12 = (f32[8,2,128]{2,1,0:T(2,128)S(1)}, f32[8,2,128]{2,1,0:T(2,128)}, u32[]{:S(2)}) copy-start(f32[8,2,128]{2,1,0:T(2,128)} %param.20) | copy-start | bytes 24580
  275.8 46.4 %copy-start.7 = (f32[8,3072]{1,0:T(8,128)S(1)}, f32[8,3072]{1,0:T(8,128)}, u32[]{:S(2)}) copy-start(f32[8,3072]{1,0:T(8,128)} %get-tuple-element.55) | copy-start | bytes 294916
  318.4 3.8 %copy-start.8 = (f32[8,3072]{1,0:T(8,128)S(1)}, f32[8,3072]{1,0:T(8,128)}, u32[]{:S(2)}) copy-start(f32[8,3072]{1,0:T(8,128)} %get-tuple-element.56) | copy-start | bytes 294916
  323.7 10.1 %collective-permute-start = (f32[8,1,128]{2,1,0:T(1,128)S(1)}, f32[8,1,128]{2,1,0:T(1,128)S(1)}, u32[]{:S(2)}, u32[]{:S(2)}) collective-permute-start(f32[8,1,128]{2,1,0:T(1,128)S(1)} %get-tuple-element.33), channel_id=1, source_target_pairs={{0,16},{16,32},{32,48},{48,64},{64,80},{80,96},{96,112},{112,128},... | collective-permute-start | bytes 12296 | tf_op jit(solution)/shard_map/ppermute | solution.py:21
  329.9 6.1 %collective-permute-start.1 = (f32[8,1,128]{2,1,0:T(1,128)S(1)}, f32[8,1,128]{2,1,0:T(1,128)S(1)}, u32[]{:S(2)}, u32[]{:S(2)}) collective-permute-start(f32[8,1,128]{2,1,0:T(1,128)S(1)} %get-tuple-element.34), channel_id=1, source_target_pairs={{16,0},{32,16},{48,32},{64,48},{80,64},{96,80},{112,96},{128,112},... | collective-permute-start | bytes 12296 | tf_op jit(solution)/shard_map/ppermute | solution.py:22
Sparse Core Ops, SparseCore 0:
  11.0 64.6 all-gather.2
  198.8 60.8 all-gather.4
where the time goes:
time: 345 us; the launch traced here: 344 us
  waiting for transfers between devices  206 us (60%)
  starting transfers between devices  36.8 us (11%)
  other arithmetic  27.1 us (8%)
  matrix products  23.7 us (7%)
  local copies, waits for them, and re-layouts  21.9 us (6%)
  between operations  15.2 us (4%)
  blocking collectives  13 us (4%)
    all_to_all x3, waiting for transfers between devices, sum_over_tensor(): parts = lax.all_to_all(parts, 'tensor', 0, 0, tiled=True)  88.7 us
    all_gather x1, waiting for transfers between devices, per_device(): piece = lax.all_gather(mlp_mod, 'tensor', axis=0, tiled=True)  52.4 us
    all_gather x1, waiting for transfers between devices, per_device(): lax.all_gather(image_mod_own, 'tensor', axis=0, tiled=True)  24.4 us
    all_to_all x1, waiting for transfers between devices, per_device(): incoming = lax.all_to_all(outgoing, 'tile', 0, 0, tiled=True)  23.7 us
    all_to_all x1, waiting for transfers between devices, per_device(): lax.all_to_all(jnp.broadcast_to(text_mod_own[None], (owners,) + text_mod_...  14.3 us
    all_to_all x3, starting transfers between devices, sum_over_tensor(): parts = lax.all_to_all(parts, 'tensor', 0, 0, tiled=True)  13.6 us
    all_to_all x1, blocking collectives, per_device(): returned = lax.all_to_all(attended_mine, 'tile', 0, 0, tiled=True)  13 us
    unnamed x50, local copies, waits for them, and re-layouts  11 us
  transfers between devices with their start and end apart: 9, of which 7 were waited for; matrix products, arithmetic and copies ran while one was open for 11% of the time, Pallas kernels for 0%

commit v1 on v0

--- a/solution.py
+++ b/solution.py
@@ -120,9 +120,9 @@
     image_count = owners * own_image
     text_tile = owners * own_text
     block_len = text_tile + image_count
-    image_mod = lax.all_gather(image_mod_own, "tensor", axis=0, tiled=True).reshape(
-        image_count * requests, model_width
-    )
+    image_mod = jnp.concatenate(
+        lax.all_to_all(jnp.stack([image_mod_own] * lax.axis_size("tensor")), "tensor", 0, 0), axis=0
+    ).reshape(image_count * requests, model_width)
     text_mod = lax.all_to_all(
         jnp.broadcast_to(text_mod_own[None], (owners,) + text_mod_own.shape),
         "tensor",

time: 345 us -> 362 us (1.049)
  waiting for transfers between devices: 206 us -> 216 us
  starting transfers between devices: 36.8 us -> 44.3 us
    all_to_all x0 -> x1, waiting for transfers between devices: none -> 28.6 us  [per_device(): lax.all_to_all(jnp.stack([image_mod_own] * lax.axis_size('tensor')), 'ten...]
    all_gather x1 -> x0, waiting for transfers between devices: 24.4 us -> none  [per_device(): lax.all_gather(image_mod_own, 'tensor', axis=0, tiled=True)]
    all_to_all x1, waiting for transfers between devices: 14.3 us -> 21.4 us  [per_device(): lax.all_to_all(jnp.broadcast_to(text_mod_own[None], (owners,) + text_mod_...]
    all_to_all x0 -> x1, starting transfers between devices: none -> 4.61 us  [per_device(): lax.all_to_all(jnp.stack([image_mod_own] * lax.axis_size('tensor')), 'ten...]
    unnamed x50 -> x38, local copies, waits for them, and re-layouts: 11 us -> 11 us
  transfers between devices with their start and end apart: 9 -> 9, of which waited for: 7 -> 7; matrix products, arithmetic and copies ran while one was open for 11% -> 10% of each run, Pallas kernels for 0% -> 0%
where the time goes in v1:
time: 362 us; the launch traced here: 361 us
  waiting for transfers between devices  216 us (60%)
  starting transfers between devices  44.3 us (12%)
  other arithmetic  26.2 us (7%)
  matrix products  23.7 us (7%)
  local copies, waits for them, and re-layouts  22.3 us (6%)
  between operations  15.2 us (4%)
  blocking collectives  13 us (4%)
    all_to_all x3, waiting for transfers between devices, sum_over_tensor(): parts = lax.all_to_all(parts, 'tensor', 0, 0, tiled=True)  89 us
    all_gather x1, waiting for transfers between devices, per_device(): piece = lax.all_gather(mlp_mod, 'tensor', axis=0, tiled=True)  51.4 us
    all_to_all x1, waiting for transfers between devices, per_device(): lax.all_to_all(jnp.stack([image_mod_own] * lax.axis_size('tensor')), 'ten...  28.6 us
    all_to_all x1, waiting for transfers between devices, per_device(): incoming = lax.all_to_all(outgoing, 'tile', 0, 0, tiled=True)  23.7 us
    all_to_all x1, waiting for transfers between devices, per_device(): lax.all_to_all(jnp.broadcast_to(text_mod_own[None], (owners,) + text_mod_...  21.4 us
    all_to_all x3, starting transfers between devices, sum_over_tensor(): parts = lax.all_to_all(parts, 'tensor', 0, 0, tiled=True)  13.6 us
    all_to_all x1, blocking collectives, per_device(): returned = lax.all_to_all(attended_mine, 'tile', 0, 0, tiled=True)  13 us
    unnamed x38, local copies, waits for them, and re-layouts  11 us
  transfers between devices with their start and end apart: 9, of which 7 were waited for; matrix products, arithmetic and copies ran while one was open for 10% of the time, Pallas kernels for 0%

profile of v1, /device:TPU:97, one launch (start us, length us, event | category | flops | bytes accessed | tf_op | source)
XLA Modules:
  0.0 361.0 jit_solution(6165897578687986220)
XLA Ops:
  7.2 1.8 slice_bitcast_fusion.4
  9.0 1.0 fusion.65
  10.0 1.1 fusion.68
  11.1 1.0 fusion.71
  12.1 1.3 broadcast_in_dim.42
  13.4 6.8 %all-to-all-start = ((bf16[16,2,8,3072]{3,2,1,0:T(8,128)(2,1)}), bf16[16,2,8,3072]{3,2,1,0:T(8,128)(2,1)}, u32[]{:S(2)}, u32[]{:S(2)}) async-start(bf16[16,2,8,3072]{3,2,1,0:T(8,128)(2,1)} %broadcast_in_dim.42), calls=%async_computation | async-start | bytes 3145728 | tf_op jit(solution)/shard_map/all_to_all | solution.py:126
  20.4 0.2 multiply_reduce_fusion
  20.7 1.0 slice_bitcast_fusion.9
  21.8 21.4 %all-to-all-done = bf16[16,2,8,3072]{3,2,1,0:T(8,128)(2,1)} async-done(((bf16[16,2,8,3072]{3,2,1,0:T(8,128)(2,1)}), bf16[16,2,8,3072]{3,2,1,0:T(8,128)(2,1)}, u32[]{:S(2)}, u32[]{:S(2)}) %all-to-all-start) | async-done | bytes 1572896 | tf_op jit(solution)/shard_map/all_to_all | solution.py:126
  43.2 2.1 stack.2
  45.2 4.6 %all-to-all-start.1 = ((bf16[16,4,8,3072]{3,2,1,0:T(8,128)(2,1)}), bf16[16,4,8,3072]{3,2,1,0:T(8,128)(2,1)}, u32[]{:S(2)}, u32[]{:S(2)}) async-start(bf16[16,4,8,3072]{3,2,1,0:T(8,128)(2,1)} %stack.2), calls=%async_computation.1 | async-start | bytes 6291456 | tf_op jit(solution)/shard_map/all_to_all | solution.py:124
  49.9 4.4 %copy.57 = bf16[3072,3,128]{0,2,1:T(8,128)(2,1)} copy(bf16[3072,3,128]{2,0,1:T(8,128)(2,1)} %param.28) | data formatting | bytes 4718592 | tf_op args[10]
  54.6 4.3 %copy.56 = bf16[3072,3,128]{0,2,1:T(8,128)(2,1)} copy(bf16[3072,3,128]{2,0,1:T(8,128)(2,1)} %param.29) | data formatting | bytes 4718592 | tf_op args[11]
  58.9 3.1 fusion.12
  62.5 0.7 copy.65
  63.4 28.6 %all-to-all-done.1 = bf16[16,4,8,3072]{3,2,1,0:T(8,128)(2,1)} async-done(((bf16[16,4,8,3072]{3,2,1,0:T(8,128)(2,1)}), bf16[16,4,8,3072]{3,2,1,0:T(8,128)(2,1)}, u32[]{:S(2)}, u32[]{:S(2)}) %all-to-all-start.1) | async-done | bytes 3145760 | tf_op jit(solution)/shard_map/all_to_all | solution.py:124
  92.0 4.0 %fusion.5 = f32[512,3,128]{0,2,1:T(8,128)S(1)} fusion(bf16[512,3072,1]{1,0,2:T(8,128)(2,1)} %bitcast.19, bf16[3072,3,128]{0,2,1:T(8,128)(2,1)} %copy.57), kind=kOutput, calls=%fused_computation.13 | convolution fusion | flops 1207959552 | bytes 6291456 | tf_op jit(solution)/shard_map/dot_general | solution.py:146
  96.3 0.7 fusion.82
  97.0 2.1 fusion.59
  99.1 0.2 copy.60
  99.3 0.9 pad_maximum_fusion.3
  100.2 0.2 copy.66
  100.4 0.7 copy.67
  101.1 0.9 pad_maximum_fusion.2
  102.4 2.0 pad_maximum_fusion
  104.4 10.8 %all-to-all-start.2 = ((bf16[16,240,1,128]{3,1,2,0:T(8,128)(2,1)}), bf16[16,240,1,128]{3,1,2,0:T(8,128)(2,1)}, u32[]{:S(2)}, u32[]{:S(2)}) async-start(bf16[16,240,1,128]{3,1,2,0:T(8,128)(2,1)} %pad_maximum_fusion), calls=%async_computation.2 | async-start | bytes 1966080 | tf_op jit(solution)/shard_map/all_to_all | solution.py:186
  115.2 0.6 dynamic_slice.3
  115.8 0.7 fusion.94
  116.5 23.7 %all-to-all-done.2 = bf16[16,240,1,128]{3,1,2,0:T(8,128)(2,1)} async-done(((bf16[16,240,1,128]{3,1,2,0:T(8,128)(2,1)}), bf16[16,240,1,128]{3,1,2,0:T(8,128)(2,1)}, u32[]{:S(2)}, u32[]{:S(2)}) %all-to-all-start.2) | async-done | bytes 983072 | tf_op jit(solution)/shard_map/all_to_all | solution.py:186
  140.1 1.2 fusion.104
  141.3 0.9 slice.176
  142.3 0.9 select_reduce_fusion
  143.1 1.1 fusion.1
  144.2 0.9 fusion.18
  145.2 13.0 %all_to_all.35 = bf16[16,48,128]{2,1,0:T(8,128)(2,1)S(1)} all-to-all(bf16[16,48,128]{2,1,0:T(8,128)(2,1)S(1)} %bitcast.210), channel_id=1, replica_groups=mesh['tile'=16,'tensor'=16] {'tile'}, dimensions={0} | all-to-all | bytes 393216 | tf_op jit(solution)/shard_map/all_to_all | solution.py:215
  158.2 0.7 copy-done.3
  158.9 2.7 convolution_convert_fusion
  161.5 4.6 %all-to-all-start.4 = ((bf16[16,4,8,3072]{3,2,1,0:T(8,128)(2,1)}), bf16[16,4,8,3072]{3,2,1,0:T(8,128)(2,1)}, u32[]{:S(2)}, u32[]{:S(2)}) async-start(bf16[16,4,8,3072]{3,2,1,0:T(8,128)(2,1)} %bitcast.190), calls=%async_computation.4 | async-start | bytes 6291456 | tf_op jit(solution)/shard_map/all_to_all | solution.py:82
  166.1 0.2 all-gather.2.cloned.1.call-start
  166.4 0.7 slice_bitcast_fusion.6
  167.1 47.2 %all-to-all-done.4 = bf16[16,4,8,3072]{3,2,1,0:T(8,128)(2,1)} async-done(((bf16[16,4,8,3072]{3,2,1,0:T(8,128)(2,1)}), bf16[16,4,8,3072]{3,2,1,0:T(8,128)(2,1)}, u32[]{:S(2)}, u32[]{:S(2)}) %all-to-all-start.4) | async-done | bytes 3145760 | tf_op jit(solution)/shard_map/all_to_all | solution.py:82
  214.3 2.5 convert_reduce_fusion.1
  217.0 0.2 fusion.41
  217.3 0.8 fusion.44
  218.1 0.5 slice.179
  219.3 3.0 fusion
  222.3 4.4 %all-to-all-start.6 = ((bf16[16,2,8,3072]{3,2,1,0:T(8,128)(2,1)}), bf16[16,2,8,3072]{3,2,1,0:T(8,128)(2,1)}, u32[]{:S(2)}, u32[]{:S(2)}) async-start(bf16[16,2,8,3072]{3,2,1,0:T(8,128)(2,1)} %bitcast.191), calls=%async_computation.6 | async-start | bytes 3145728 | tf_op jit(solution)/shard_map/all_to_all | solution.py:82
  226.7 51.4 %all-gather.2.cloned.1.call-done = bf16[64,8,3072]{2,1,0:T(8,128)(2,1)} async-done(((bf16[4,8,3072]{2,1,0:T(8,128)(2,1)}), bf16[64,8,3072]{2,1,0:T(8,128)(2,1)}) %all-gather.2.cloned.1.call-update) | async-done | bytes 3145744 | tf_op jit(solution)/shard_map/all_gather | solution.py:232
  278.1 7.8 %convolution_convert_fusion.1 = bf16[512,3072]{1,0:T(8,128)(2,1)} fusion(bf16[384,3072]{1,0:T(8,128)(2,1)S(1)} %copy-done, bf16[3072,384]{1,0:T(8,128)(2,1)} %param.33, bf16[64,8,3072]{2,1,0:T(8,128)(2,1)} %all-gather.2.cloned.1.call-done), kind=kOutput, calls=%fused_computation.5 | convolution fusion | flops 2419261440 | bytes 11010048 | tf_op jit(solution)/shard_map/dot_general | solution.py:238
  285.9 4.6 %all-to-all-start.5 = ((bf16[16,4,8,3072]{3,2,1,0:T(8,128)(2,1)}), bf16[16,4,8,3072]{3,2,1,0:T(8,128)(2,1)}, u32[]{:S(2)}, u32[]{:S(2)}) async-start(bf16[16,4,8,3072]{3,2,1,0:T(8,128)(2,1)} %bitcast.192), calls=%async_computation.5 | async-start | bytes 6291456 | tf_op jit(solution)/shard_map/all_to_all | solution.py:82
  290.6 1.2 fusion.109
  291.8 0.7 copy_bitcast_fusion
  292.5 1.6 convert_reduce_fusion.2
  294.2 0.7 copy.74
  294.9 41.8 %all-to-all-done.5 = bf16[16,4,8,3072]{3,2,1,0:T(8,128)(2,1)} async-done(((bf16[16,4,8,3072]{3,2,1,0:T(8,128)(2,1)}), bf16[16,4,8,3072]{3,2,1,0:T(8,128)(2,1)}, u32[]{:S(2)}, u32[]{:S(2)}) %all-to-all-start.5) | async-done | bytes 3145760 | tf_op jit(solution)/shard_map/all_to_all | solution.py:82
  336.7 2.5 convert_reduce_fusion
  339.4 0.2 fusion.45
  339.7 1.3 convolution_bitcast_fusion
  341.2 6.2 %collective-permute-start = (f32[8,1,128]{2,1,0:T(1,128)S(1)}, f32[8,1,128]{2,1,0:T(1,128)S(1)}, u32[]{:S(2)}, u32[]{:S(2)}) collective-permute-start(f32[8,1,128]{2,1,0:T(1,128)S(1)} %get-tuple-element.33), channel_id=1, source_target_pairs={{0,16},{16,32},{32,48},{48,64},{64,80},{80,96},{96,112},{112,128},... | collective-permute-start | bytes 12296 | tf_op jit(solution)/shard_map/ppermute | solution.py:21
  347.4 1.9 collective-permute-start.1
  349.3 1.1 fusion.51
  350.4 0.9 copy.73
  351.3 2.3 collective-permute-done.1
  353.5 0.6 pad_maximum_fusion.4
  (88 shorter events, 2.5 us)
Async XLA Ops:
  7.2 270.9 %copy-start = (bf16[384,3072]{1,0:T(8,128)(2,1)S(1)}, bf16[384,3072]{1,0:T(8,128)(2,1)}, u32[]{:S(2)}) copy-start(bf16[384,3072]{1,0:T(8,128)(2,1)} %param.34) | copy-start | bytes 7077892
  7.2 13.1 %copy-start.11 = (bf16[8,2,2,3072]{3,2,1,0:T(2,128)(2,1)S(1)}, bf16[8,2,2,3072]{3,2,1,0:T(2,128)(2,1)}, u32[]{:S(2)}) copy-start(bf16[8,2,2,3072]{3,2,1,0:T(2,128)(2,1)} %param.18) | copy-start | bytes 589828
  13.4 29.7 %all-to-all-start = ((bf16[16,2,8,3072]{3,2,1,0:T(8,128)(2,1)}), bf16[16,2,8,3072]{3,2,1,0:T(8,128)(2,1)}, u32[]{:S(2)}, u32[]{:S(2)}) async-start(bf16[16,2,8,3072]{3,2,1,0:T(8,128)(2,1)} %broadcast_in_dim.42), calls=%async_computation | async-start | bytes 3145728 | tf_op jit(solution)/shard_map/all_to_all | solution.py:126
  45.2 46.7 %all-to-all-start.1 = ((bf16[16,4,8,3072]{3,2,1,0:T(8,128)(2,1)}), bf16[16,4,8,3072]{3,2,1,0:T(8,128)(2,1)}, u32[]{:S(2)}, u32[]{:S(2)}) async-start(bf16[16,4,8,3072]{3,2,1,0:T(8,128)(2,1)} %stack.2), calls=%async_computation.1 | async-start | bytes 6291456 | tf_op jit(solution)/shard_map/all_to_all | solution.py:124
  49.9 4.4 %copy-start.14 = (s32[8,2]{0,1:T(2,128)S(1)}, s32[8,2]{0,1:T(2,128)}, u32[]{:S(2)}) copy-start(s32[8,2]{0,1:T(2,128)} %param.22) | copy-start | bytes 196
  54.2 4.7 %copy-start.13 = (f32[2,2,128]{2,1,0:T(2,128)S(1)}, f32[2,2,128]{2,1,0:T(2,128)}, u32[]{:S(2)}) copy-start(f32[2,2,128]{2,1,0:T(2,128)} %param.32) | copy-start | bytes 6148
  101.1 14.1 %copy-start.15 = (s32[8]{0:T(128)S(1)}, s32[8]{0:T(128)}, u32[]{:S(2)}) copy-start(s32[8]{0:T(128)} %param.23) | copy-start | bytes 100
  104.4 35.8 %all-to-all-start.2 = ((bf16[16,240,1,128]{3,1,2,0:T(8,128)(2,1)}), bf16[16,240,1,128]{3,1,2,0:T(8,128)(2,1)}, u32[]{:S(2)}, u32[]{:S(2)}) async-start(bf16[16,240,1,128]{3,1,2,0:T(8,128)(2,1)} %pad_maximum_fusion), calls=%async_computation.2 | async-start | bytes 1966080 | tf_op jit(solution)/shard_map/all_to_all | solution.py:186
  144.2 14.6 %copy-start.4 = (bf16[128,3072]{1,0:T(8,128)(2,1)S(1)}, bf16[128,3072]{1,0:T(8,128)(2,1)}, u32[]{:S(2)}) copy-start(bf16[128,3072]{1,0:T(8,128)(2,1)} %param.30) | copy-start | bytes 2359300
  158.2 0.7 copy-start.3
  161.5 4.8 %copy-start.10 = (f32[8,3,3072]{2,0,1:T(8,128)S(1)}, f32[8,3,3072]{2,0,1:T(8,128)}, u32[]{:S(2)}) copy-start(f32[8,3,3072]{2,0,1:T(8,128)} %param.26) | copy-start | bytes 884740
  161.5 52.8 %all-to-all-start.4 = ((bf16[16,4,8,3072]{3,2,1,0:T(8,128)(2,1)}), bf16[16,4,8,3072]{3,2,1,0:T(8,128)(2,1)}, u32[]{:S(2)}, u32[]{:S(2)}) async-start(bf16[16,4,8,3072]{3,2,1,0:T(8,128)(2,1)} %bitcast.190), calls=%async_computation.4 | async-start | bytes 6291456 | tf_op jit(solution)/shard_map/all_to_all | solution.py:82
  166.1 111.9 %all-gather.2.cloned.1.call-start = ((), (), s32[]{:S(2)}) async-start(), calls=%async_computation.7 | async-start | bytes 3342336 | tf_op jit(solution)/shard_map/all_gather | solution.py:232
  214.3 3.0 copy-start.5
  214.3 3.0 copy-start.6
  216.9 5.4 %copy-start.1 = (f32[4,8,3072]{2,1,0:T(8,128)}, f32[4,8,3072]{2,1,0:T(8,128)S(1)}, u32[]{:S(2)}) copy-start(f32[4,8,3072]{2,1,0:T(8,128)S(1)} %convert_reduce_fusion.1) | copy-start | bytes 1179652
  222.3 63.6 %all-to-all-start.6 = ((bf16[16,2,8,3072]{3,2,1,0:T(8,128)(2,1)}), bf16[16,2,8,3072]{3,2,1,0:T(8,128)(2,1)}, u32[]{:S(2)}, u32[]{:S(2)}) async-start(bf16[16,2,8,3072]{3,2,1,0:T(8,128)(2,1)} %bitcast.191), calls=%async_computation.6 | async-start | bytes 3145728 | tf_op jit(solution)/shard_map/all_to_all | solution.py:82
  285.9 4.7 %copy-start.16 = (s32[8]{0:T(128)S(1)}, s32[8]{0:T(128)}, u32[]{:S(2)}) copy-start(s32[8]{0:T(128)} %param.21) | copy-start | bytes 100
  285.9 8.3 %copy-start.2 = (bf16[8,2,3072]{2,1,0:T(2,128)(2,1)S(1)}, bf16[8,2,3072]{2,1,0:T(2,128)(2,1)}, u32[]{:S(2)}) copy-start(bf16[8,2,3072]{2,1,0:T(2,128)(2,1)} %param.19) | copy-start | bytes 294916
  285.9 8.3 %copy-start.9 = (f32[8,3072]{1,0:T(8,128)S(1)}, f32[8,3072]{1,0:T(8,128)}, u32[]{:S(2)}) copy-start(f32[8,3072]{1,0:T(8,128)} %get-tuple-element.14) | copy-start | bytes 294916
  285.9 50.8 %all-to-all-start.5 = ((bf16[16,4,8,3072]{3,2,1,0:T(8,128)(2,1)}), bf16[16,4,8,3072]{3,2,1,0:T(8,128)(2,1)}, u32[]{:S(2)}, u32[]{:S(2)}) async-start(bf16[16,4,8,3072]{3,2,1,0:T(8,128)(2,1)} %bitcast.192), calls=%async_computation.5 | async-start | bytes 6291456 | tf_op jit(solution)/shard_map/all_to_all | solution.py:82
  294.1 46.9 %copy-start.12 = (f32[8,2,128]{2,1,0:T(2,128)S(1)}, f32[8,2,128]{2,1,0:T(2,128)}, u32[]{:S(2)}) copy-start(f32[8,2,128]{2,1,0:T(2,128)} %param.20) | copy-start | bytes 24580
  336.7 2.9 copy-start.7
  336.7 2.9 copy-start.8
  341.2 10.1 %collective-permute-start = (f32[8,1,128]{2,1,0:T(1,128)S(1)}, f32[8,1,128]{2,1,0:T(1,128)S(1)}, u32[]{:S(2)}, u32[]{:S(2)}) collective-permute-start(f32[8,1,128]{2,1,0:T(1,128)S(1)} %get-tuple-element.33), channel_id=1, source_target_pairs={{0,16},{16,32},{32,48},{48,64},{64,80},{80,96},{96,112},{112,128},... | collective-permute-start | bytes 12296 | tf_op jit(solution)/shard_map/ppermute | solution.py:21
  347.4 6.1 %collective-permute-start.1 = (f32[8,1,128]{2,1,0:T(1,128)S(1)}, f32[8,1,128]{2,1,0:T(1,128)S(1)}, u32[]{:S(2)}, u32[]{:S(2)}) collective-permute-start(f32[8,1,128]{2,1,0:T(1,128)S(1)} %get-tuple-element.34), channel_id=1, source_target_pairs={{16,0},{32,16},{48,32},{64,48},{80,64},{96,80},{112,96},{128,112},... | collective-permute-start | bytes 12296 | tf_op jit(solution)/shard_map/ppermute | solution.py:22
Sparse Core Ops, SparseCore 0:
  218.2 59.8 all-gather.1
